TPU v7x, 32 devices: a whole 2x2x4 slice. The times are simulated.
32 devices in a mesh: dp: 4 (over z), space: 4 (over x, core), rep: 2 (over y).
Axes of the slice: x: 2, y: 2, z: 4, core: 2. Of those that a mesh axis runs over, the one named last changes fastest.
Arguments:
- frames: bfloat16 [6, 8, 32, 32, 512], P(None, ('dp', 'rep'), 'space'), may hold values from -6 to 6
- membrane: bfloat16 [8, 32, 32, 512], P(('dp', 'rep'), 'space'), may hold values from -6 to 6
- cotangent: bfloat16 [6, 8, 32, 32, 512], P(None, ('dp', 'rep'), 'space'), may hold values from -6 to 6
- master: float32 [4608, 512], P('dp'), may hold values from -0.09375 to 0.09375
- moment: float32 [4608, 512], P('dp'), may hold values from -4 to 4
- second: float32 [4608, 512], P('dp'), may hold values from 0.05 to 5
Outputs:
- grad_input: bfloat16 [6, 8, 32, 32, 512], P(None, ('dp', 'rep'), 'space')
- membrane_grad: float32 [8, 32, 32, 512], P(('dp', 'rep'), 'space')
- weight_grad: float32 [4608, 512], P('dp')
- new_moment: float32 [4608, 512], P('dp')
- new_second: float32 [4608, 512], P('dp')
- update: float32 [4608, 512], P('dp')
All inputs are finite; a program needn't handle non-finite values.
Results may differ from a plain program's by a relative error of at most 0.003.
Values may be sent and summed in bfloat16 or wider, within the bound.
No kernel may reach another device: no remote copies, remote signals or barrier semaphores. Data moves between devices by JAX's collectives and lax.ppermute only.
A program may use at most 192 MiB of HBM per device.

v0:
```python
import math
import jax
import jax.numpy as jnp
from jax import lax
from jax.sharding import PartitionSpec as P


def extended(x, sides, width):
    for axis, dim in sides:
        peers, length = (lax.axis_size(axis), x.shape[dim])
        up = [(i, (i + 1) % peers) for i in range(peers - 1)]
        down = [(j, i) for i, j in up]
        last = lax.slice_in_dim(x, length - width, length, axis=dim)
        first = lax.slice_in_dim(x, 0, width, axis=dim)
        before = lax.ppermute(last, axis, up)
        after = lax.ppermute(first, axis, down)
        x = jnp.concatenate([before, x, after], axis=dim)
    return x


def surrogate(potential):
    return 1.0 / (1.0 + (math.pi * (potential - 1.0)) ** 2)


def offsets_list():
    return [(row_shift, col_shift) for row_shift in (-1, 0, 1) for col_shift in (-1, 0, 1)]


def on_device(frames, membrane, cotangent, master, moment, second):
    steps_count, samples, rows, cols, chans = frames.shape
    weights = lax.all_gather(master.astype(jnp.bfloat16), "dp", axis=0, tiled=True)
    stacked = jnp.concatenate([membrane[None], frames], axis=0)
    rimmed = extended(stacked, (("space", 2),), 1)
    voltage = rimmed[0].astype(jnp.float32)
    potentials = []
    fired = []
    for position in range(steps_count):
        potential = 0.5 * voltage + rimmed[position + 1].astype(jnp.float32)
        spikes = jnp.where(potential >= 1.0, jnp.float32(1.0), jnp.float32(0.0))
        voltage = potential - spikes
        potentials.append(potential[:, 1:-1])
        fired.append(spikes)
    potential_all = jnp.stack(potentials)
    spike_all = jnp.stack(fired).astype(jnp.bfloat16)
    col_pad = ((0, 0), (0, 0), (0, 0), (1, 1), (0, 0))
    spike_pad = jnp.pad(spike_all, col_pad)
    grad_rim = extended(cotangent, (("space", 2),), 1)
    grad_pad = jnp.pad(grad_rim, col_pad)
    spike_cols = jnp.concatenate(
        [spike_pad[:, :, 1 + a : 1 + a + rows, 1 + b : 1 + b + cols] for a, b in offsets_list()],
        axis=-1,
    ).reshape(-1, 9 * chans)
    grad_cols = jnp.concatenate(
        [grad_pad[:, :, 1 - a : 1 - a + rows, 1 - b : 1 - b + cols] for a, b in offsets_list()],
        axis=-1,
    ).reshape(-1, 9, chans)
    grad_flat = cotangent.reshape(-1, chans)
    weight_local = lax.dot_general(
        spike_cols, grad_flat, (((0,), (0,)), ((), ())), preferred_element_type=jnp.float32
    )
    dspikes = jnp.einsum(
        "nkd,kcd->nc",
        grad_cols,
        weights.reshape(9, chans, chans),
        preferred_element_type=jnp.float32,
    )
    dspikes = dspikes.reshape(steps_count, samples, rows, cols, chans)
    carried = jnp.zeros((samples, rows, cols, chans), jnp.float32)
    outs = [None] * steps_count
    for position in reversed(range(steps_count)):
        carried = dspikes[position] * surrogate(potential_all[position]) + 0.5 * carried
        outs[position] = (cotangent[position].astype(jnp.float32) + carried).astype(jnp.bfloat16)
    grad_input = jnp.stack(outs)
    membrane_grad = 0.5 * carried
    data_count = lax.axis_size("dp")
    total_cells = samples * data_count * lax.axis_size("rep") * rows * lax.axis_size("space") * cols
    shard_part = lax.psum_scatter(weight_local, "dp", scatter_dimension=0, tiled=True)
    summed = lax.psum(shard_part, ("space", "rep"))
    weight_grad = summed * (1.0 / math.sqrt(steps_count * total_cells))
    new_moment = 0.9 * moment + 0.1 * weight_grad
    new_second = 0.95 * second + 0.05 * weight_grad * weight_grad
    update = new_moment / (jnp.sqrt(new_second) + 1e-08)
    return (grad_input, membrane_grad, weight_grad, new_moment, new_second, update)


def solution(mesh):
    return jax.shard_map(
        on_device,
        mesh=mesh,
        in_specs=(
            P(None, ("dp", "rep"), "space", None, None),
            P(("dp", "rep"), "space", None, None),
            P(None, ("dp", "rep"), "space", None, None),
            P("dp", None),
            P("dp", None),
            P("dp", None),
        ),
        out_specs=(
            P(None, ("dp", "rep"), "space", None, None),
            P(("dp", "rep"), "space", None, None),
            P("dp", None),
            P("dp", None),
            P("dp", None),
            P("dp", None),
        ),
        check_vma=False,
    )
```

profile of v0, /device:TPU:0, one launch (start us, length us, event | category | flops | bytes accessed | tf_op | source)
XLA Modules:
  0.0 351.5 jit_solution(18133478292274602957)
XLA Ops:
  7.2 1.1 pad_maximum_fusion.4
  8.3 1.3 collective-permute-start.3
  9.6 3.2 collective-permute-start.2
  12.8 2.8 convert_element_type.357
  15.7 1.8 pad_maximum_fusion
  24.6 10.2 %fusion.4 = f32[4608,512]{1,0:T(8,128)} fusion(bf16[6,1,8,32,4608]{4,3,2,0,1:T(8,128)(2,1)S(1)} %fusion.21, bf16[6,1,8,32,512]{4,3,2,1,0:T(8,128)(2,1)S(1)} %copy-done), kind=kOutput, calls=%fused_computation.4 | convolution fusion | flops 7247757312 | bytes 25165824 | tf_op jit(solution)/shard_map/dot_general | solution.py:58
  34.8 1.1 fusion.104
  35.9 1.3 collective-permute-start.1
  37.2 5.5 %collective-permute-start = (bf16[6,1,1,32,512]{4,3,2,1,0:T(8,128)(2,1)S(1)}, bf16[6,1,1,32,512]{4,3,2,1,0:T(8,128)(2,1)S(1)}, u32[]{:S(2)}, u32[]{:S(2)}) collective-permute-start(bf16[6,1,1,32,512]{4,3,2,1,0:T(8,128)(2,1)S(1)} %get-tuple-element.29), channel_id=1, source_target_pairs={{0,2},{2,4},{4,6},{1,3},{3,5},{5,7},{8,10},{10,12},{12,14},{9,11},... | collective-permute-start | bytes 589832 | tf_op jit(solution)/shard_map/ppermute | solution.py:15
  42.7 0.8 collective-permute-done
  43.5 2.3 fusion.15
  45.9 1.7 slice_dynamic-update-slice_fusion.8
  47.5 1.4 fusion.23
  49.0 1.4 slice_dynamic-update-slice_fusion.7
  50.4 2.1 slice_dynamic-update-slice_fusion.6
  52.5 1.4 constant_dynamic-update-slice_fusion
  53.8 1.4 slice_dynamic-update-slice_fusion.5
  55.2 2.0 slice_dynamic-update-slice_fusion.4
  57.2 1.4 fusion.22
  58.6 1.4 slice_dynamic-update-slice_fusion.3
  60.0 26.6 %reshape.515 = bf16[1536,9,512]{2,1,0:T(8,128)(2,1)} reshape(bf16[6,1,8,32,4608]{4,3,2,1,0:T(8,128)(2,1)} %slice_dynamic-update-slice_fusion.3) | data formatting | bytes 28311552 | tf_op jit(solution)/shard_map/reshape | solution.py:56
  86.6 1.0 fusion.73
  87.6 0.9 convert_bitcast_fusion.1
  88.6 1.8 fusion.28
  90.4 17.5 %all-gather.2.cloned.1.call-done = bf16[4608,512]{1,0:T(8,128)(2,1)} async-done(((bf16[1152,512]{1,0:T(8,128)(2,1)}), bf16[4608,512]{1,0:T(8,128)(2,1)}) %all-gather.2.cloned.1.call-update) | async-done | bytes 4718608 | tf_op jit(solution)/shard_map/all_gather | solution.py:31
  107.9 25.8 %fusion.8 = f32[1536,512]{1,0:T(8,128)S(1)} fusion(bf16[9,512,512]{2,1,0:T(8,128)(2,1)} %bitcast.158, bf16[1536,9,512]{2,1,0:T(8,128)(2,1)} %reshape.515), kind=kOutput, calls=%fused_computation.8 | convolution fusion | flops 7247757312 | bytes 22020096 | tf_op jit(solution)/shard_map/nkd,kcd->nc/dot_general | solution.py:61
  135.8 1.7 broadcast_multiply_fusion.1
  138.3 131.7 %reduce-scatter.2.cloned.1.call-done = f32[1152,512]{1,0:T(8,128)} async-done(((f32[4608,512]{1,0:T(8,128)}), f32[1152,512]{1,0:T(8,128)}) %reduce-scatter.2.cloned.1.call-update) | async-done | bytes 2359312 | tf_op jit(solution)/shard_map/reduce_scatter | solution.py:77
  270.1 2.2 fusion.87
  273.9 0.9 fusion.93
  275.6 61.5 %all-reduce.4.cloned.1.call-done = f32[1152,512]{1,0:T(8,128)} async-done(((f32[1152,512]{1,0:T(8,128)}), f32[1152,512]{1,0:T(8,128)}) %all-reduce.4.cloned.1.call-update) | async-done | bytes 2359312 | tf_op jit(solution)/shard_map/psum | solution.py:78
  337.1 7.9 %add_divide_fusion = (f32[1152,512]{1,0:T(8,128)}, f32[1152,512]{1,0:T(8,128)}, f32[1152,512]{1,0:T(8,128)}, f32[1152,512]{1,0:T(8,128)}) fusion(f32[1152,512]{1,0:T(8,128)} %all-reduce.4.cloned.1.call-done, f32[1152,512]{1,0:T(8,128)} %param.11, f32[1152,512]{1,0:T(8,128)} %param.10), kind=kLoop, calls=%fused_computation.14 | loop fusion | flops 5898240 | bytes 16515072 | tf_op jit(solution)/shard_map/div | solution.py:82
  (55 shorter events, 12.3 us)
Async XLA Ops:
  7.2 100.7 %all-gather.2.cloned.1.call-start = ((), (), s32[]{:S(2)}) async-start(), calls=%async_computation.1 | async-start | bytes 5898240 | tf_op jit(solution)/shard_map/all_gather | solution.py:31
  8.3 7.4 %collective-permute-start.3 = (bf16[7,1,1,32,512]{4,3,2,1,0:T(8,128)(2,1)S(1)}, bf16[7,1,1,32,512]{4,3,2,1,0:T(8,128)(2,1)S(1)}, u32[]{:S(2)}, u32[]{:S(2)}) collective-permute-start(bf16[7,1,1,32,512]{4,3,2,1,0:T(8,128)(2,1)S(1)} %get-tuple-element.28), channel_id=1, source_target_pairs={{2,0},{4,2},{6,4},{3,1},{5,3},{7,5},{10,8},{12,10},{14,12},{11,9},... | collective-permute-start | bytes 688136 | tf_op jit(solution)/shard_map/ppermute | solution.py:16
  9.6 6.1 %copy-start.12 = (bf16[1,8,32,512]{3,2,1,0:T(8,128)(2,1)S(1)}, bf16[1,8,32,512]{3,2,1,0:T(8,128)(2,1)}, u32[]{:S(2)}) copy-start(bf16[1,8,32,512]{3,2,1,0:T(8,128)(2,1)} %param.7) | copy-start | bytes 786436
  9.6 6.1 %collective-permute-start.2 = (bf16[7,1,1,32,512]{4,3,2,1,0:T(8,128)(2,1)S(1)}, bf16[7,1,1,32,512]{4,3,2,1,0:T(8,128)(2,1)S(1)}, u32[]{:S(2)}, u32[]{:S(2)}) collective-permute-start(bf16[7,1,1,32,512]{4,3,2,1,0:T(8,128)(2,1)S(1)} %get-tuple-element.27), channel_id=1, source_target_pairs={{0,2},{2,4},{4,6},{1,3},{3,5},{5,7},{8,10},{10,12},{12,14},{9,11},... | collective-permute-start | bytes 688136 | tf_op jit(solution)/shard_map/ppermute | solution.py:15
  15.6 254.4 %reduce-scatter.2.cloned.1.call-start = ((), (), s32[]{:S(2)}) async-start(), calls=%async_computation.2 | async-start | bytes 11796480 | tf_op jit(solution)/shard_map/reduce_scatter | solution.py:77
  23.2 1.4 copy-start
  34.8 302.3 %all-reduce.4.cloned.1.call-start = ((), (), s32[]{:S(2)}) async-start(), calls=%async_computation.3 | async-start | bytes 4718592 | tf_op jit(solution)/shard_map/psum | solution.py:78
  35.9 6.8 %collective-permute-start.1 = (bf16[6,1,1,32,512]{4,3,2,1,0:T(8,128)(2,1)S(1)}, bf16[6,1,1,32,512]{4,3,2,1,0:T(8,128)(2,1)S(1)}, u32[]{:S(2)}, u32[]{:S(2)}) collective-permute-start(bf16[6,1,1,32,512]{4,3,2,1,0:T(8,128)(2,1)S(1)} %get-tuple-element.30), channel_id=1, source_target_pairs={{2,0},{4,2},{6,4},{3,1},{5,3},{7,5},{10,8},{12,10},{14,12},{11,9},... | collective-permute-start | bytes 589832 | tf_op jit(solution)/shard_map/ppermute | solution.py:16
  37.2 6.3 %collective-permute-start = (bf16[6,1,1,32,512]{4,3,2,1,0:T(8,128)(2,1)S(1)}, bf16[6,1,1,32,512]{4,3,2,1,0:T(8,128)(2,1)S(1)}, u32[]{:S(2)}, u32[]{:S(2)}) collective-permute-start(bf16[6,1,1,32,512]{4,3,2,1,0:T(8,128)(2,1)S(1)} %get-tuple-element.29), channel_id=1, source_target_pairs={{0,2},{2,4},{4,6},{1,3},{3,5},{5,7},{8,10},{10,12},{12,14},{9,11},... | collective-permute-start | bytes 589832 | tf_op jit(solution)/shard_map/ppermute | solution.py:15
  45.8 1.7 copy-start.1
  133.7 1.1 copy-start.4
  133.7 1.3 copy-start.6
  133.7 1.5 copy-start.7
  133.8 1.7 copy-start.8
  133.8 1.8 copy-start.9
  133.8 2.0 copy-start.10
  135.8 1.7 copy-start.2
  270.1 2.3 copy-start.3
  270.1 3.0 copy-start.11
  270.1 3.8 %copy-start.5 = (f32[1,10,32,512]{3,2,1,0:T(8,128)S(1)}, f32[1,10,32,512]{3,2,1,0:T(8,128)}, u32[]{:S(2)}) copy-start(f32[1,10,32,512]{3,2,1,0:T(8,128)} %get-tuple-element.17) | copy-start | bytes 1966084
Sparse Core Ops, SparseCore 0:
  15.8 92.1 all-gather.1
  110.3 159.7 reduce-scatter.1
  273.3 63.7 all-reduce.3
where the time goes:
time: 353 us; the launch traced here: 352 us
  waiting for transfers between devices  212 us (60%)
  local copies, waits for them, and re-layouts  46.2 us (13%)
  matrix products  36 us (10%)
  other arithmetic  32.3 us (9%)
  between operations  14.1 us (4%)
  starting transfers between devices  11.3 us (3%)
    reduce_scatter x1, waiting for transfers between devices, on_device(): lax.psum_scatter(weight_local, 'dp', scatter_dimension=0, tiled=True)  132 us
    psum x1, waiting for transfers between devices, on_device(): summed = lax.psum(shard_part, ('space', 'rep'))  61.5 us
    reshape x1, local copies, waits for them, and re-layouts, on_device(): grad_cols = jnp.concatenate([grad_pad[:, :, 1 - a:1 - a + rows, 1 - b:1 -...  26.6 us
    dot_general x1, matrix products, on_device(): jnp.einsum('nkd,kcd->nc', grad_cols, weights.reshape(9, chans, chans), pr...  25.8 us
    all_gather x1, waiting for transfers between devices, on_device(): lax.all_gather(master.astype(jnp.bfloat16), 'dp', axis=0, tiled=True)  17.5 us
    unnamed x40, local copies, waits for them, and re-layouts  16.1 us
    dot_general x1, matrix products, on_device(): lax.dot_general(spike_cols, grad_flat, (((0,), (0,)), ((), ())), preferre...  10.2 us
    unnamed x12, other arithmetic  9.82 us
  transfers between devices with their start and end apart: 7, of which 4 were waited for; matrix products, arithmetic and copies ran while one was open for 29% of the time, Pallas kernels for 0%

commit v1 on v0

--- a/solution.py
+++ b/solution.py
@@ -3,6 +3,10 @@
 import jax.numpy as jnp
 from jax import lax
 from jax.sharding import PartitionSpec as P
+
+
+def rows_note(array_in):
+    return lax.psum(lax.psum(array_in, axis_name="rep"), "space")
 
 
 def extended(x, sides, width):
@@ -75,7 +79,7 @@
     data_count = lax.axis_size("dp")
     total_cells = samples * data_count * lax.axis_size("rep") * rows * lax.axis_size("space") * cols
     shard_part = lax.psum_scatter(weight_local, "dp", scatter_dimension=0, tiled=True)
-    summed = lax.psum(shard_part, ("space", "rep"))
+    summed = rows_note(shard_part)
     weight_grad = summed * (1.0 / math.sqrt(steps_count * total_cells))
     new_moment = 0.9 * moment + 0.1 * weight_grad
     new_second = 0.95 * second + 0.05 * weight_grad * weight_grad

time: 353 us -> 435 us (1.23)
  waiting for transfers between devices: 212 us -> 294 us
    all_gather x1, waiting for transfers between devices: 17.5 us -> 92.4 us  [on_device(): lax.all_gather(master.astype(jnp.bfloat16), 'dp', axis=0, tiled=True)]
    psum x1 -> x2, waiting for transfers between devices: 61.5 us -> 91.7 us  [rows_note(): return lax.psum(lax.psum(array_in, axis_name='rep'), 'space')]
    reduce_scatter x1, waiting for transfers between devices: 132 us -> 108 us  [on_device(): lax.psum_scatter(weight_local, 'dp', scatter_dimension=0, tiled=True)]
    unnamed x40 -> x42, local copies, waits for them, and re-layouts: 16.1 us -> 16 us
  transfers between devices with their start and end apart: 7 -> 8, of which waited for: 4 -> 6; matrix products, arithmetic and copies ran while one was open for 29% -> 19% of each run, Pallas kernels for 0% -> 0%
where the time goes in v1:
time: 435 us; the launch traced here: 434 us
  waiting for transfers between devices  294 us (68%)
  local copies, waits for them, and re-layouts  46.2 us (11%)
  matrix products  35.8 us (8%)
  other arithmetic  31 us (7%)
  between operations  14.1 us (3%)
  starting transfers between devices  12.9 us (3%)
    reduce_scatter x1, waiting for transfers between devices, on_device(): lax.psum_scatter(weight_local, 'dp', scatter_dimension=0, tiled=True)  108 us
    all_gather x1, waiting for transfers between devices, on_device(): lax.all_gather(master.astype(jnp.bfloat16), 'dp', axis=0, tiled=True)  92.4 us
    psum x2, waiting for transfers between devices, rows_note(): return lax.psum(lax.psum(array_in, axis_name='rep'), 'space')  91.7 us
    reshape x1, local copies, waits for them, and re-layouts, on_device(): grad_cols = jnp.concatenate([grad_pad[:, :, 1 - a:1 - a + rows, 1 - b:1 -...  26.6 us
    dot_general x1, matrix products, on_device(): jnp.einsum('nkd,kcd->nc', grad_cols, weights.reshape(9, chans, chans), pr...  25.6 us
    unnamed x42, local copies, waits for them, and re-layouts  16 us
    dot_general x1, matrix products, on_device(): lax.dot_general(spike_cols, grad_flat, (((0,), (0,)), ((), ())), preferre...  10.2 us
    ppermute x2, starting transfers between devices, extended(): before = lax.ppermute(last, axis, up)  10.2 us
  transfers between devices with their start and end apart: 8, of which 6 were waited for; matrix products, arithmetic and copies ran while one was open for 19% of the time, Pallas kernels for 0%

profile of v1, /device:TPU:0, one launch (start us, length us, event | category | flops | bytes accessed | tf_op | source)
XLA Modules:
  0.0 433.8 jit_solution(415623557436342763)
XLA Ops:
  7.2 1.2 pad_maximum_fusion.4
  8.4 1.3 collective-permute-start.3
  9.7 3.0 collective-permute-start.2
  12.8 1.1 collective-permute-done.2
  21.3 10.2 %fusion.4 = f32[4608,512]{1,0:T(8,128)} fusion(bf16[6,1,8,32,4608]{4,3,2,0,1:T(8,128)(2,1)S(1)} %fusion.21, bf16[6,1,8,32,512]{4,3,2,1,0:T(8,128)(2,1)S(1)} %copy-done), kind=kOutput, calls=%fused_computation.4 | convolution fusion | flops 7247757312 | bytes 25165824 | tf_op jit(solution)/shard_map/dot_general | solution.py:62
  31.6 2.8 convert_element_type.357
  34.5 1.1 fusion.104
  35.5 1.3 collective-permute-start.1
  36.8 7.1 %collective-permute-start = (bf16[6,1,1,32,512]{4,3,2,1,0:T(8,128)(2,1)S(1)}, bf16[6,1,1,32,512]{4,3,2,1,0:T(8,128)(2,1)S(1)}, u32[]{:S(2)}, u32[]{:S(2)}) collective-permute-start(bf16[6,1,1,32,512]{4,3,2,1,0:T(8,128)(2,1)S(1)} %get-tuple-element.29), channel_id=1, source_target_pairs={{0,2},{2,4},{4,6},{1,3},{3,5},{5,7},{8,10},{10,12},{12,14},{9,11},... | collective-permute-start | bytes 589832 | tf_op jit(solution)/shard_map/ppermute | solution.py:19
  44.8 2.4 fusion.15
  47.2 1.7 slice_dynamic-update-slice_fusion.8
  48.9 1.5 fusion.23
  50.4 1.4 slice_dynamic-update-slice_fusion.7
  51.8 2.0 slice_dynamic-update-slice_fusion.6
  53.7 1.4 constant_dynamic-update-slice_fusion
  55.1 1.4 slice_dynamic-update-slice_fusion.5
  56.6 2.0 slice_dynamic-update-slice_fusion.4
  58.5 1.4 fusion.22
  59.9 1.5 slice_dynamic-update-slice_fusion.3
  61.4 26.6 %reshape.515 = bf16[1536,9,512]{2,1,0:T(8,128)(2,1)} reshape(bf16[6,1,8,32,4608]{4,3,2,1,0:T(8,128)(2,1)} %slice_dynamic-update-slice_fusion.3) | data formatting | bytes 28311552 | tf_op jit(solution)/shard_map/reshape | solution.py:60
  88.0 0.9 fusion.73
  88.9 0.9 convert_bitcast_fusion.1
  89.8 1.8 fusion.28
  91.7 107.8 %reduce-scatter.2.cloned.1.call-done = f32[1152,512]{1,0:T(8,128)} async-done(((f32[4608,512]{1,0:T(8,128)}), f32[1152,512]{1,0:T(8,128)}) %reduce-scatter.2.cloned.1.call-update) | async-done | bytes 2359312 | tf_op jit(solution)/shard_map/reduce_scatter | solution.py:81
  199.6 92.4 %all-gather.2.cloned.1.call-done = bf16[4608,512]{1,0:T(8,128)(2,1)} async-done(((bf16[1152,512]{1,0:T(8,128)(2,1)}), bf16[4608,512]{1,0:T(8,128)(2,1)}) %all-gather.2.cloned.1.call-update) | async-done | bytes 4718608 | tf_op jit(solution)/shard_map/all_gather | solution.py:35
  291.9 25.6 %fusion.8 = f32[1536,512]{1,0:T(8,128)S(1)} fusion(bf16[9,512,512]{2,1,0:T(8,128)(2,1)} %bitcast.158, bf16[1536,9,512]{2,1,0:T(8,128)(2,1)} %reshape.515), kind=kOutput, calls=%fused_computation.8 | convolution fusion | flops 7247757312 | bytes 22020096 | tf_op jit(solution)/shard_map/nkd,kcd->nc/dot_general | solution.py:65
  319.6 1.7 broadcast_multiply_fusion.1
  322.1 39.2 %all-reduce.5.cloned.1.call-done = f32[1152,512]{1,0:T(8,128)} async-done(((f32[1152,512]{1,0:T(8,128)}), f32[1152,512]{1,0:T(8,128)}) %all-reduce.5.cloned.1.call-update) | async-done | bytes 2359312 | tf_op jit(solution)/shard_map/psum | solution.py:9
  361.4 2.2 fusion.87
  365.2 0.9 fusion.93
  366.8 52.5 %all-reduce.7.cloned.1.call-done = f32[1152,512]{1,0:T(8,128)} async-done(((f32[1152,512]{1,0:T(8,128)}), f32[1152,512]{1,0:T(8,128)}) %all-reduce.7.cloned.1.call-update) | async-done | bytes 2359312 | tf_op jit(solution)/shard_map/psum | solution.py:9
  419.3 7.9 %add_divide_fusion = (f32[1152,512]{1,0:T(8,128)}, f32[1152,512]{1,0:T(8,128)}, f32[1152,512]{1,0:T(8,128)}, f32[1152,512]{1,0:T(8,128)}) fusion(f32[1152,512]{1,0:T(8,128)} %all-reduce.7.cloned.1.call-done, f32[1152,512]{1,0:T(8,128)} %param.11, f32[1152,512]{1,0:T(8,128)} %param.10), kind=kLoop, calls=%fused_computation.14 | loop fusion | flops 5898240 | bytes 16515072 | tf_op jit(solution)/shard_map/div | solution.py:86
  (60 shorter events, 13.6 us)
Async XLA Ops:
  7.2 6.7 %copy-start.13 = (bf16[1,8,32,512]{3,2,1,0:T(8,128)(2,1)S(1)}, bf16[1,8,32,512]{3,2,1,0:T(8,128)(2,1)}, u32[]{:S(2)}) copy-start(bf16[1,8,32,512]{3,2,1,0:T(8,128)(2,1)} %param.7) | copy-start | bytes 786436
  7.2 192.3 %reduce-scatter.2.cloned.1.call-start = ((), (), s32[]{:S(2)}) async-start(), calls=%async_computation.2 | async-start | bytes 11796480 | tf_op jit(solution)/shard_map/reduce_scatter | solution.py:81
  7.2 6.6 %copy-start.3 = (bf16[6,1,8,32,512]{4,3,2,1,0:T(8,128)(2,1)S(1)}, bf16[6,1,8,32,512]{4,3,2,1,0:T(8,128)(2,1)}, u32[]{:S(2)}) copy-start(bf16[6,1,8,32,512]{4,3,2,1,0:T(8,128)(2,1)} %param.6) | copy-start | bytes 4718596
  8.4 4.4 %collective-permute-start.3 = (bf16[7,1,1,32,512]{4,3,2,1,0:T(8,128)(2,1)S(1)}, bf16[7,1,1,32,512]{4,3,2,1,0:T(8,128)(2,1)S(1)}, u32[]{:S(2)}, u32[]{:S(2)}) collective-permute-start(bf16[7,1,1,32,512]{4,3,2,1,0:T(8,128)(2,1)S(1)} %get-tuple-element.28), channel_id=1, source_target_pairs={{2,0},{4,2},{6,4},{3,1},{5,3},{7,5},{10,8},{12,10},{14,12},{11,9},... | collective-permute-start | bytes 688136 | tf_op jit(solution)/shard_map/ppermute | solution.py:20
  9.7 4.1 collective-permute-start.2
  19.9 1.4 copy-start
  31.5 260.4 %all-gather.2.cloned.1.call-start = ((), (), s32[]{:S(2)}) async-start(), calls=%async_computation.1 | async-start | bytes 5898240 | tf_op jit(solution)/shard_map/all_gather | solution.py:35
  34.4 326.9 %all-reduce.5.cloned.1.call-start = ((), (), s32[]{:S(2)}) async-start(), calls=%async_computation.3 | async-start | bytes 4718592 | tf_op jit(solution)/shard_map/psum | solution.py:9
  35.5 8.4 %collective-permute-start.1 = (bf16[6,1,1,32,512]{4,3,2,1,0:T(8,128)(2,1)S(1)}, bf16[6,1,1,32,512]{4,3,2,1,0:T(8,128)(2,1)S(1)}, u32[]{:S(2)}, u32[]{:S(2)}) collective-permute-start(bf16[6,1,1,32,512]{4,3,2,1,0:T(8,128)(2,1)S(1)} %get-tuple-element.30), channel_id=1, source_target_pairs={{2,0},{4,2},{6,4},{3,1},{5,3},{7,5},{10,8},{12,10},{14,12},{11,9},... | collective-permute-start | bytes 589832 | tf_op jit(solution)/shard_map/ppermute | solution.py:20
  36.8 8.0 %collective-permute-start = (bf16[6,1,1,32,512]{4,3,2,1,0:T(8,128)(2,1)S(1)}, bf16[6,1,1,32,512]{4,3,2,1,0:T(8,128)(2,1)S(1)}, u32[]{:S(2)}, u32[]{:S(2)}) collective-permute-start(bf16[6,1,1,32,512]{4,3,2,1,0:T(8,128)(2,1)S(1)} %get-tuple-element.29), channel_id=1, source_target_pairs={{0,2},{2,4},{4,6},{1,3},{3,5},{5,7},{8,10},{10,12},{12,14},{9,11},... | collective-permute-start | bytes 589832 | tf_op jit(solution)/shard_map/ppermute | solution.py:19
  47.2 1.7 copy-start.1
  199.5 219.8 %all-reduce.7.cloned.1.call-start = ((), (), s32[]{:S(2)}) async-start(), calls=%async_computation.4 | async-start | bytes 4718592 | tf_op jit(solution)/shard_map/psum | solution.py:9
  317.5 1.1 copy-start.5
  317.5 1.3 copy-start.7
  317.5 1.5 copy-start.8
  317.5 1.7 copy-start.9
  317.5 1.8 copy-start.10
  317.6 2.0 copy-start.11
  319.6 1.7 copy-start.2
  361.3 2.3 copy-start.4
  361.3 3.0 copy-start.12
  361.4 3.8 copy-start.6
Sparse Core Ops, SparseCore 0:
  31.6 167.7 reduce-scatter.1
  201.6 90.2 all-gather.1
  294.2 67.0 all-reduce.4
  363.7 55.6 all-reduce.6
